TPU v7x, 256 devices: a whole 4x4x8 slice. The times are simulated.
256 devices in a mesh: cfg: 2 (over z_lo), req: 16 (over y, z_hi), mlp: 8 (over x, core).
Axes of the slice: x: 4, y: 4, z: 8 (z_hi: 4, z_lo: 2; z = z_hi * 2 + z_lo), core: 2. Of those that a mesh axis runs over, the one named last changes fastest.
Arguments:
- hidden: bfloat16 [2, 16384, 1152], P('cfg', ('req', 'mlp')), may hold values from -64 to 64
- noisy_latent: float32 [16384, 16], P(('req', 'mlp'), 'cfg'), may hold values from -6 to 6
- labels: int32 [16, 4], replicated, may hold values from 0 to 999
- timesteps: int32 [16, 4], replicated, may hold values from 0 to 999
- lengths: int32 [16, 4], P('req'), may hold values from 1 to 512, 1024 in all within a row
- guidance: float32 [16, 4], P('req'), may hold values from 1.5 to 4
- keep_scale: float32 [16, 4], P('req'), may hold values from 0.9 to 1.2
- noise_scale: float32 [16, 4], P('req'), may hold values from -0.8 to -0.2
- class_table: bfloat16 [1001, 1152], replicated, may hold values from -6 to 6
- time_up: bfloat16 [256, 1152], replicated, may hold values from -0.375 to 0.375
- time_up_bias: bfloat16 [1152], replicated, may hold values from -4 to 4
- time_out: bfloat16 [1152, 1152], replicated, may hold values from -0.1875 to 0.1875
- time_out_bias: bfloat16 [1152], replicated, may hold values from -4 to 4
- mod_weight: bfloat16 [1152, 9216], P(None, 'req'), may hold values from -0.1875 to 0.1875
- mod_bias: bfloat16 [9216], P('req'), may hold values from -4 to 4
- qkv_weight: bfloat16 [1152, 3456], P(None, 'req'), may hold values from -8 to 8
- qkv_bias: bfloat16 [3456], P('req'), may hold values from -4 to 4
- out_weight: bfloat16 [1152, 1152], P(None, 'req'), may hold values from -0.1875 to 0.1875
- out_bias: bfloat16 [1152], P('req'), may hold values from -4 to 4
- up_weight: bfloat16 [1152, 4608], P(None, 'mlp'), may hold values from -0.1875 to 0.1875
- up_bias: bfloat16 [4608], P('mlp'), may hold values from -4 to 4
- down_weight: bfloat16 [4608, 1152], P('mlp'), may hold values from -1 to 1
- down_bias: bfloat16 [1152], replicated, may hold values from -4 to 4
- final_weight: bfloat16 [1152, 16], replicated, may hold values from -0.1875 to 0.1875
- final_bias: bfloat16 [16], replicated, may hold values from -4 to 4
Outputs:
- next_latent: float32 [16384, 16], P(('req', 'mlp'), 'cfg')
Inputs may be any that keep to these rules, and one draw needn't show every extreme that they name: `lengths`: each row sums to 1024, and its largest crop has exactly 512 tokens.
All inputs are finite; a program needn't handle non-finite values.
Results may differ from a plain program's by a relative error of at most 0.015.
Values may be sent and summed in bfloat16 or wider, within the bound.
No kernel may reach another device: no remote copies, remote signals or barrier semaphores. Data moves between devices by JAX's collectives and lax.ppermute only.
A program may use at most 128 MiB of HBM per device.

v0:
```python
import math
import jax
import jax.numpy as jnp
from jax import lax
from jax.sharding import PartitionSpec as P

HEADS = 16
HEAD_DIM = 72
CLASSES = 1000
FREQ = 256


def layer_norm(values):
    values = values.astype(jnp.float32)
    centre = values - jnp.mean(values, axis=-1, keepdims=True)
    variance = jnp.mean(centre * centre, axis=-1, keepdims=True)
    return centre * lax.rsqrt(variance + 1e-06)


def time_features(times_flat):
    half_freq = FREQ // 2
    frequency = jnp.exp(-math.log(10000.0) * jnp.arange(half_freq, dtype=jnp.float32) / half_freq)
    angles = times_flat.astype(jnp.float32)[:, None] * frequency[None, :]
    return jnp.concatenate([jnp.cos(angles), jnp.sin(angles)], axis=1).astype(jnp.bfloat16)


def segment_ids(lengths_row, positions):
    ends = jnp.cumsum(lengths_row)
    return jnp.sum((positions[:, None] >= ends[None, :]).astype(jnp.int32), axis=1)


def attention(queries, keys_all, values_all, query_segment, key_segment):
    scores = jnp.einsum(
        "qhd,khd->hqk", queries, keys_all, preferred_element_type=jnp.float32
    ) / math.sqrt(HEAD_DIM)
    same = (query_segment[:, None] == key_segment[None, :])[None]
    masked = jnp.where(same, scores, -1e30)
    row_max = jnp.max(masked, axis=2, keepdims=True)
    expo = jnp.where(same, jnp.exp(masked - row_max), 0.0)
    denominator = jnp.sum(expo, axis=2)
    weights = expo.astype(jnp.bfloat16)
    mixed = jnp.einsum("hqk,khd->qhd", weights, values_all, preferred_element_type=jnp.float32)
    result = mixed / jnp.transpose(denominator)[:, :, None]
    return result.astype(jnp.bfloat16).reshape(queries.shape[0], -1)


def shards(
    hidden,
    noisy_latent,
    labels,
    timesteps,
    lengths,
    guidance,
    keep_scale,
    noise_scale,
    class_table,
    time_up,
    time_up_bias,
    time_out,
    time_out_bias,
    mod_weight,
    mod_bias,
    qkv_weight,
    qkv_bias,
    out_weight,
    out_bias,
    up_weight,
    up_bias,
    down_weight,
    down_bias,
    final_weight,
    final_bias,
):
    req_count = lax.axis_size("req")
    mlp_count = lax.axis_size("mlp")
    half_index = lax.axis_index("cfg")
    mlp_index = lax.axis_index("mlp")
    tok_rows = hidden.shape[1]
    width = hidden.shape[2]
    group_rows = tok_rows * mlp_count
    per_group = labels.shape[1]
    time_feat = time_features(timesteps.reshape(-1))
    time_mid = jax.nn.silu(
        jnp.dot(time_feat, time_up, preferred_element_type=jnp.float32)
        + time_up_bias.astype(jnp.float32)
    ).astype(jnp.bfloat16)
    time_cond = jnp.dot(
        time_mid, time_out, preferred_element_type=jnp.float32
    ) + time_out_bias.astype(jnp.float32)
    used_labels = jnp.where(half_index == 0, labels.reshape(-1), CLASSES)
    one_hot = (used_labels[:, None] == jnp.arange(CLASSES + 1, dtype=jnp.int32)[None, :]).astype(
        jnp.bfloat16
    )
    cond_act = jax.nn.silu(
        time_cond + jnp.dot(one_hot, class_table, preferred_element_type=jnp.float32)
    ).astype(jnp.bfloat16)
    local_mod = (
        jnp.dot(cond_act, mod_weight, preferred_element_type=jnp.float32)
        + mod_bias.astype(jnp.float32)
    ).astype(jnp.bfloat16)
    local_mod = local_mod.reshape(req_count, per_group, local_mod.shape[1])
    modulation = lax.all_to_all(local_mod, "req", split_axis=0, concat_axis=2, tiled=True)[0]
    positions = jnp.arange(group_rows, dtype=jnp.int32)
    segment_all = segment_ids(lengths[0], positions)
    segment_own = lax.dynamic_slice_in_dim(segment_all, mlp_index * tok_rows, tok_rows)
    member = segment_own[:, None] == jnp.arange(per_group, dtype=jnp.int32)[None, :]
    per_token = jnp.dot(member.astype(jnp.bfloat16), modulation, preferred_element_type=jnp.float32)
    pieces = [per_token[:, index * width : (index + 1) * width] for index in range(8)]
    shift_attn, scale_attn, gate_attn, shift_mlp, scale_mlp, gate_mlp, shift_final, scale_final = (
        pieces
    )
    rows = hidden[0]
    normed = (layer_norm(rows) * (1.0 + scale_attn) + shift_attn).astype(jnp.bfloat16)
    core = mlp_index % 2
    half_rows = width // 2
    pair = [(index, index ^ 1) for index in range(mlp_count)]

    def split_gather(weight, bias):
        mine = lax.dynamic_slice_in_dim(weight, core * half_rows, half_rows, axis=0)
        bias_rows = jnp.zeros((16, weight.shape[1]), weight.dtype).at[0].set(bias)
        gathered = lax.all_gather(
            jnp.concatenate([mine, bias_rows], axis=0), "req", axis=1, tiled=True
        )
        return (gathered, lax.ppermute(gathered, "mlp", pair))

    def split_dot(values, mine, other):
        values_mine = lax.dynamic_slice_in_dim(values, core * half_rows, half_rows, axis=1)
        values_other = lax.dynamic_slice_in_dim(values, (1 - core) * half_rows, half_rows, axis=1)
        return (
            jnp.dot(values_mine, mine[:half_rows], preferred_element_type=jnp.float32)
            + jnp.dot(values_other, other[:half_rows], preferred_element_type=jnp.float32)
            + mine[half_rows].astype(jnp.float32)
        )

    qkv_mine, qkv_other = split_gather(qkv_weight, qkv_bias)
    out_mine, out_other = split_gather(out_weight, out_bias)
    qkv = split_dot(normed, qkv_mine, qkv_other).astype(jnp.bfloat16)
    heads_per = HEADS // mlp_count
    head_cols = heads_per * HEAD_DIM
    packed = jnp.transpose(qkv.reshape(tok_rows, 3, mlp_count, head_cols), (0, 2, 1, 3)).reshape(
        tok_rows, mlp_count * 3 * head_cols
    )
    own_heads = lax.all_to_all(packed, "mlp", split_axis=1, concat_axis=0, tiled=True)
    attended_heads = attention(
        own_heads[:, :head_cols].reshape(group_rows, heads_per, HEAD_DIM),
        own_heads[:, head_cols : 2 * head_cols].reshape(group_rows, heads_per, HEAD_DIM),
        own_heads[:, 2 * head_cols :].reshape(group_rows, heads_per, HEAD_DIM),
        segment_all,
        segment_all,
    )
    attended = lax.all_to_all(attended_heads, "mlp", split_axis=0, concat_axis=1, tiled=True)
    projected = split_dot(attended, out_mine, out_other)
    mid_hidden = (rows.astype(jnp.float32) + gate_attn * projected).astype(jnp.bfloat16)
    normed_mlp = (layer_norm(mid_hidden) * (1.0 + scale_mlp) + shift_mlp).astype(jnp.bfloat16)
    gathered = lax.all_gather(normed_mlp, "mlp", axis=0, tiled=True)
    inner = jax.nn.gelu(
        jnp.dot(gathered, up_weight, preferred_element_type=jnp.float32)
        + up_bias.astype(jnp.float32),
        approximate=True,
    ).astype(jnp.bfloat16)
    mlp_out = lax.psum_scatter(
        jnp.dot(inner, down_weight, preferred_element_type=jnp.float32).astype(jnp.bfloat16),
        "mlp",
        scatter_dimension=0,
        tiled=True,
    ).astype(jnp.float32)
    final_hidden = mid_hidden.astype(jnp.float32) + gate_mlp * (
        mlp_out + down_bias.astype(jnp.float32)
    )
    normed_final = (layer_norm(final_hidden) * (1.0 + scale_final) + shift_final).astype(
        jnp.bfloat16
    )
    predicted = jnp.dot(
        normed_final, final_weight, preferred_element_type=jnp.float32
    ) + final_bias.astype(jnp.float32)
    halves = lax.all_to_all(predicted[None], "cfg", split_axis=2, concat_axis=0, tiled=True)
    eps_cond = halves[0]
    eps_free = halves[1]
    member_f = member.astype(jnp.float32)
    guide_tok = jnp.sum(member_f * guidance, axis=1, keepdims=True)
    keep_tok = jnp.sum(member_f * keep_scale, axis=1, keepdims=True)
    noise_tok = jnp.sum(member_f * noise_scale, axis=1, keepdims=True)
    return keep_tok * noisy_latent + noise_tok * (eps_free + guide_tok * (eps_cond - eps_free))


def solution(mesh):
    return jax.shard_map(
        shards,
        mesh=mesh,
        in_specs=(
            P("cfg", ("req", "mlp"), None),
            P(("req", "mlp"), "cfg"),
            P(),
            P(),
            P("req", None),
            P("req", None),
            P("req", None),
            P("req", None),
            P(),
            P(),
            P(),
            P(),
            P(),
            P(None, "req"),
            P("req"),
            P(None, "req"),
            P("req"),
            P(None, "req"),
            P("req"),
            P(None, "mlp"),
            P("mlp"),
            P("mlp", None),
            P(),
            P(),
            P(),
        ),
        out_specs=P(("req", "mlp"), "cfg"),
        check_vma=False,
    )
```

profile of v0, /device:TPU:8, one launch (start us, length us, event | category | flops | bytes accessed | tf_op | source)
XLA Modules:
  0.0 295.6 jit_solution(11914430172864486977)
XLA Ops:
  6.5 0.9 reshape.215
  7.4 1.1 constant_dynamic-slice_fusion.1
  8.6 0.8 fusion.54
  9.4 0.0 all-gather.4.cloned.1.call-update
  9.5 79.9 %all-gather.4.cloned.1.call-done = bf16[592,3456]{0,1:T(8,128)(2,1)} async-done(((bf16[592,216]{0,1:T(8,128)(2,1)}), bf16[592,3456]{0,1:T(8,128)(2,1)}) %all-gather.4.cloned.1.call-update) | async-done | bytes 4091920 | tf_op jit(solution)/shard_map/all_gather | solution.py:121
  89.3 7.0 %copy.82 = bf16[592,3456]{1,0:T(8,128)(2,1)} copy(bf16[592,3456]{0,1:T(8,128)(2,1)} %all-gather.4.cloned.1.call-done) | data formatting | bytes 8183808 | tf_op jit(solution)/shard_map/all_gather | solution.py:121
  96.4 0.1 copy.78
  96.4 0.1 convert_element_type.93
  96.6 0.1 copy.79
  96.7 0.1 select_n.45
  96.8 0.2 fusion.66
  97.0 1.8 convolution_add_fusion.3
  98.9 3.0 %fusion.37 = bf16[64,576]{1,0:T(8,128)(2,1)S(1)} fusion(bf16[1152,576]{0,1:T(8,128)(2,1)} %param.42, f32[64,1152]{1,0:T(8,128)S(1)} %convolution_add_fusion.3, bf16[1001,1152]{1,0:T(8,128)(2,1)} %param.37, s32[64]{0:T(128)S(1)} %select_n.45, f32[576]{0:T(1024)S(1)} %convert_element_type.98), kind=kOutput, calls=%fused_computation.43 | convolution fusion | flops 233118272 | bytes 4004608 | tf_op jit(solution)/shard_map/dot_general | solution.py:98
  101.9 0.6 reshape.206
  102.6 9.5 %all-to-all-start = ((bf16[16,4,576]{2,1,0:T(4,128)(2,1)}), bf16[16,4,576]{2,1,0:T(4,128)(2,1)S(1)}, u32[]{:S(2)}, u32[]{:S(2)}) async-start(bf16[16,4,576]{2,1,0:T(4,128)(2,1)} %reshape.206), calls=%async_computation | async-start | bytes 163840 | tf_op jit(solution)/shard_map/all_to_all | solution.py:102
  112.1 0.0 all-gather.6.cloned.1.call-start
  112.1 0.1 copy.94
  112.2 0.1 constant_dynamic-slice_fusion
  112.4 0.7 fusion.65
  113.1 0.2 reduce-window.8
  113.3 0.1 convert_reduce_fusion.3
  113.4 0.1 dynamic_slice.21
  113.5 0.1 convert_reduce_fusion.1
  113.6 0.2 fusion.43
  113.8 6.9 %all-to-all-done = bf16[16,4,576]{2,1,0:T(4,128)(2,1)S(1)} async-done(((bf16[16,4,576]{2,1,0:T(4,128)(2,1)}), bf16[16,4,576]{2,1,0:T(4,128)(2,1)S(1)}, u32[]{:S(2)}, u32[]{:S(2)}) %all-to-all-start) | async-done | bytes 73760 | tf_op jit(solution)/shard_map/all_to_all | solution.py:102
  120.8 0.1 squeeze.6
  120.9 0.8 fusion.79
  121.8 2.1 copy-done.1
  123.9 0.3 fusion.46
  124.1 1.8 convert_reduce_fusion
  125.9 3.7 %fusion.4 = f32[128,3456]{1,0:T(8,128)S(1)} fusion(bf16[592,3456]{0,1:T(8,128)(2,1)} %all-gather.4.cloned.1.call-done, bf16[128,1152]{1,0:T(8,128)(2,1)S(1)} %fusion.46, s32[]{:T(128)S(6)} %select_n.47), kind=kOutput, calls=%fused_computation.7 | convolution fusion | flops 509607936 | bytes 6025220 | tf_op jit(solution)/shard_map/dot_general | solution.py:130
  129.7 4.0 %fusion.3 = bf16[128,3456]{1,0:T(8,128)(2,1)} fusion(f32[128,3456]{1,0:T(8,128)S(1)} %fusion.4, bf16[592,3456]{1,0:T(8,128)(2,1)} %collective-permute-done, f32[3456]{0:T(1024)S(1)} %convert_reduce_fusion, bf16[128,1152]{1,0:T(8,128)(2,1)S(1)} %fusion.46, s32[]{:T(128)S(6)} %select_n.48), kind=kOutput, calls=%fused_computation.6 | convolution fusion | flops 510935040 | bytes 6815748 | tf_op jit(solution)/shard_map/dot_general | solution.py:131
  133.7 2.2 copy.83
  136.0 2.2 copy.84
  138.1 4.2 %all-to-all-start.1 = ((bf16[128,8,432]{0,2,1:T(8,128)(2,1)}), bf16[128,8,432]{0,2,1:T(8,128)(2,1)}, u32[]{:S(2)}, u32[]{:S(2)}) async-start(bf16[128,8,432]{0,2,1:T(8,128)(2,1)} %bitcast.96), calls=%async_computation.1 | async-start | bytes 1769472 | tf_op jit(solution)/shard_map/all_to_all | solution.py:143
  142.4 1.6 broadcast_compare_fusion
  144.0 26.4 %all-gather.6.cloned.1.call-done = bf16[592,1152]{0,1:T(8,128)(2,1)} async-done(((bf16[592,72]{0,1:T(8,128)(2,1)}), bf16[592,1152]{0,1:T(8,128)(2,1)}) %all-gather.6.cloned.1.call-update) | async-done | bytes 1363984 | tf_op jit(solution)/shard_map/all_gather | solution.py:121
  170.4 3.6 %copy.89 = bf16[592,1152]{1,0:T(8,128)(2,1)} copy(bf16[592,1152]{0,1:T(8,128)(2,1)} %all-gather.6.cloned.1.call-done) | data formatting | bytes 2727936 | tf_op jit(solution)/shard_map/all_gather | solution.py:121
  174.0 1.3 copy_bitcast_fusion
  175.3 0.8 fusion.98
  176.1 8.4 %fusion.99 = (f32[2,1024]{1,0:T(2,128)S(1)}, bf16[2,1024,1024]{1,2,0:T(8,128)(2,1)}) fusion(pred[1024,1024]{0,1:T(8,128)(4,1)} %broadcast_compare_fusion, bf16[1024,2,72]{0,2,1:T(8,128)(2,1)} %bitcast.104, bf16[1024,2,72]{0,2,1:T(8,128)(2,1)S(1)} %bitcast.103), kind=kOutput, calls=%fused_computation.135 | convolution fusion | flops 314573824 | bytes 5840896 | tf_op jit(solution)/shard_map/sub | solution.py:39
  184.5 3.0 %fusion.34 = bf16[1024,2,72]{0,2,1:T(8,128)(2,1)S(1)} fusion(bf16[1024,2,72]{0,2,1:T(8,128)(2,1)S(1)} %bitcast.102, bf16[2,1024,1024]{1,2,0:T(8,128)(2,1)} %get-tuple-element.40, f32[1024,2]{0,1:T(2,128)S(1)} %bitcast.113), kind=kOutput, calls=%fused_computation.41 | convolution fusion | flops 302284800 | bytes 4792320 | tf_op jit(solution)/shard_map/hqk,khd->qhd/dot_general | solution.py:42
  187.5 0.1 copy.96
  187.6 0.7 copy.87
  188.3 4.2 %all-to-all-start.2 = ((bf16[8,128,144]{1,2,0:T(8,128)(2,1)}), bf16[8,128,144]{1,2,0:T(8,128)(2,1)S(1)}, u32[]{:S(2)}, u32[]{:S(2)}) async-start(bf16[8,128,144]{1,2,0:T(8,128)(2,1)} %copy.87), calls=%async_computation.2 | async-start | bytes 589824 | tf_op jit(solution)/shard_map/all_to_all | solution.py:151
  192.6 0.0 all-gather.8.cloned.1.call-start
  192.6 1.2 convert_reduce_fusion.2
  193.8 6.6 %all-to-all-done.2 = bf16[8,128,144]{1,2,0:T(8,128)(2,1)S(1)} async-done(((bf16[8,128,144]{1,2,0:T(8,128)(2,1)}), bf16[8,128,144]{1,2,0:T(8,128)(2,1)S(1)}, u32[]{:S(2)}, u32[]{:S(2)}) %all-to-all-start.2) | async-done | bytes 294944 | tf_op jit(solution)/shard_map/all_to_all | solution.py:151
  200.4 2.1 fusion.25
  202.5 2.1 fusion.100
  204.6 0.2 multiply_reduce_fusion.1
  204.8 2.2 fusion.49
  207.0 0.0 reduce-scatter.2.cloned.1.call-start
  207.1 25.0 %all-gather.8.cloned.1.call-done = bf16[1024,1152]{1,0:T(8,128)(2,1)} async-done(((bf16[128,1152]{1,0:T(8,128)(2,1)}), bf16[1024,1152]{1,0:T(8,128)(2,1)}) %all-gather.8.cloned.1.call-update) | async-done | bytes 2359312 | tf_op jit(solution)/shard_map/all_gather | solution.py:155
  232.1 7.9 %convolution_convert_fusion = bf16[1024,1152]{1,0:T(8,128)(2,1)} fusion(bf16[576,1152]{1,0:T(8,128)(2,1)} %param.50, bf16[1024,1152]{1,0:T(8,128)(2,1)} %all-gather.8.cloned.1.call-done, bf16[1152,576]{0,1:T(8,128)(2,1)} %param.48, f32[576]{0:T(1024)S(1)} %convert_element_type.107), kind=kOutput, calls=%fused_computation.15 | convolution fusion | flops 2724986880 | bytes 7375104 | tf_op jit(solution)/shard_map/dot_general | solution.py:162
  240.0 0.7 copy-done.8
  240.7 37.0 %reduce-scatter.2.cloned.1.call-done = bf16[128,1152]{1,0:T(8,128)(2,1)} async-done(((bf16[1024,1152]{1,0:T(8,128)(2,1)}), bf16[128,1152]{1,0:T(8,128)(2,1)}) %reduce-scatter.2.cloned.1.call-update) | async-done | bytes 294928 | tf_op jit(solution)/shard_map/reduce_scatter | solution.py:161
  277.7 1.3 fusion.96
  279.0 0.2 multiply_reduce_fusion
  279.3 2.2 convolution_add_fusion.6
  281.4 3.2 %all-to-all-start.3 = ((f32[1,128,16]{1,0,2:T(1,128)}), f32[1,128,16]{1,0,2:T(1,128)S(1)}, u32[]{:S(2)}, u32[]{:S(2)}) async-start(f32[1,128,16]{1,0,2:T(1,128)} %bitcast.21), calls=%async_computation.4 | async-start | bytes 16384 | tf_op jit(solution)/shard_map/all_to_all | solution.py:176
  284.7 0.1 select_reduce_fusion.2
  284.8 3.7 %all-to-all-done.3 = f32[1,128,16]{1,0,2:T(1,128)S(1)} async-done(((f32[1,128,16]{1,0,2:T(1,128)}), f32[1,128,16]{1,0,2:T(1,128)S(1)}, u32[]{:S(2)}, u32[]{:S(2)}) %all-to-all-start.3) | async-done | bytes 8224 | tf_op jit(solution)/shard_map/all_to_all | solution.py:176
  288.4 0.6 fusion.78
  (63 shorter events, 0.3 us)
Async XLA Ops:
  6.5 90.5 %copy-start = (bf16[1152,1152]{1,0:T(8,128)(2,1)S(1)}, bf16[1152,1152]{1,0:T(8,128)(2,1)}, u32[]{:S(2)}) copy-start(bf16[1152,1152]{1,0:T(8,128)(2,1)} %param.40) | copy-start | bytes 7962628
  6.5 82.8 %all-gather.4.cloned.1.call-start = ((), (), s32[]{:S(2)}) async-start(), calls=%async_computation.5 | async-start | bytes 4700160 | tf_op jit(solution)/shard_map/all_gather | solution.py:121
  9.4 87.0 %copy-start.12 = (s32[16,4]{0,1:T(4,128)S(1)}, s32[16,4]{0,1:T(4,128)}, u32[]{:S(2)}) copy-start(s32[16,4]{0,1:T(4,128)} %param.32) | copy-start | bytes 772
  9.4 87.1 %copy-start.6 = (bf16[1152]{0:T(1024)(128)(2,1)S(1)}, bf16[1152]{0:T(1024)(128)(2,1)}, u32[]{:S(2)}) copy-start(bf16[1152]{0:T(1024)(128)(2,1)} %param.39) | copy-start | bytes 6916
  9.4 87.1 %copy-start.7 = (bf16[1152]{0:T(1024)(128)(2,1)S(1)}, bf16[1152]{0:T(1024)(128)(2,1)}, u32[]{:S(2)}) copy-start(bf16[1152]{0:T(1024)(128)(2,1)} %param.41) | copy-start | bytes 6916
  9.4 87.1 %copy-start.13 = (s32[16,4]{0,1:T(4,128)S(1)}, s32[16,4]{0,1:T(4,128)}, u32[]{:S(2)}) copy-start(s32[16,4]{0,1:T(4,128)} %param.31) | copy-start | bytes 772
  9.4 87.3 %copy-start.10 = (bf16[576]{0:T(1024)(128)(2,1)S(1)}, bf16[576]{0:T(1024)(128)(2,1)}, u32[]{:S(2)}) copy-start(bf16[576]{0:T(1024)(128)(2,1)} %param.43) | copy-start | bytes 3460
  96.3 33.3 %collective-permute-start = (bf16[592,3456]{1,0:T(8,128)(2,1)}, bf16[592,3456]{1,0:T(8,128)(2,1)}, u32[]{:S(2)}, u32[]{:S(2)}) collective-permute-start(bf16[592,3456]{1,0:T(8,128)(2,1)} %copy.82), channel_id=1, source_target_pairs={{0,1},{1,0},{2,3},{3,2},{4,5},{5,4},{6,7},{7,6},{8,9},{9,8},{10,11... | collective-permute-start | bytes 12275720 | tf_op jit(solution)/shard_map/ppermute | solution.py:124
  98.8 13.3 %copy-start.14 = (bf16[72]{0:T(256)(128)(2,1)S(1)}, bf16[72]{0:T(256)(128)(2,1)}, u32[]{:S(2)}) copy-start(bf16[72]{0:T(256)(128)(2,1)} %param.47) | copy-start | bytes 436
  98.8 13.4 %copy-start.4 = (bf16[1152,72]{0,1:T(8,128)(2,1)S(1)}, bf16[1152,72]{0,1:T(8,128)(2,1)}, u32[]{:S(2)}) copy-start(bf16[1152,72]{0,1:T(8,128)(2,1)} %param.46) | copy-start | bytes 497668
  98.9 14.3 %copy-start.18 = (s32[1,4]{1,0:T(1,128)S(1)}, s32[1,4]{1,0:T(1,128)}, u32[]{:S(2)}) copy-start(s32[1,4]{1,0:T(1,128)} %param.33) | copy-start | bytes 52
  98.9 14.6 %copy-start.2 = (bf16[1,128,1152]{2,1,0:T(8,128)(2,1)S(1)}, bf16[1,128,1152]{2,1,0:T(8,128)(2,1)}, u32[]{:S(2)}) copy-start(bf16[1,128,1152]{2,1,0:T(8,128)(2,1)} %param.29) | copy-start | bytes 884740
  102.6 18.2 %all-to-all-start = ((bf16[16,4,576]{2,1,0:T(4,128)(2,1)}), bf16[16,4,576]{2,1,0:T(4,128)(2,1)S(1)}, u32[]{:S(2)}, u32[]{:S(2)}) async-start(bf16[16,4,576]{2,1,0:T(4,128)(2,1)} %reshape.206), calls=%async_computation | async-start | bytes 163840 | tf_op jit(solution)/shard_map/all_to_all | solution.py:102
  112.1 58.3 %all-gather.6.cloned.1.call-start = ((), (), s32[]{:S(2)}) async-start(), calls=%async_computation.6 | async-start | bytes 1566720 | tf_op jit(solution)/shard_map/all_gather | solution.py:121
  121.7 2.1 copy-start.1
  138.1 35.9 %all-to-all-start.1 = ((bf16[128,8,432]{0,2,1:T(8,128)(2,1)}), bf16[128,8,432]{0,2,1:T(8,128)(2,1)}, u32[]{:S(2)}, u32[]{:S(2)}) async-start(bf16[128,8,432]{0,2,1:T(8,128)(2,1)} %bitcast.96), calls=%async_computation.1 | async-start | bytes 1769472 | tf_op jit(solution)/shard_map/all_to_all | solution.py:143
  174.0 28.5 %collective-permute-start.1 = (bf16[592,1152]{1,0:T(8,128)(2,1)}, bf16[592,1152]{1,0:T(8,128)(2,1)}, u32[]{:S(2)}, u32[]{:S(2)}) collective-permute-start(bf16[592,1152]{1,0:T(8,128)(2,1)} %copy.89), channel_id=1, source_target_pairs={{0,1},{1,0},{2,3},{3,2},{4,5},{5,4},{6,7},{7,6},{8,9},{9,8},{10,11... | collective-permute-start | bytes 4091912 | tf_op jit(solution)/shard_map/ppermute | solution.py:124
  188.3 12.1 %all-to-all-start.2 = ((bf16[8,128,144]{1,2,0:T(8,128)(2,1)}), bf16[8,128,144]{1,2,0:T(8,128)(2,1)S(1)}, u32[]{:S(2)}, u32[]{:S(2)}) async-start(bf16[8,128,144]{1,2,0:T(8,128)(2,1)} %copy.87), calls=%async_computation.2 | async-start | bytes 589824 | tf_op jit(solution)/shard_map/all_to_all | solution.py:151
  192.6 39.5 %all-gather.8.cloned.1.call-start = ((), (), s32[]{:S(2)}) async-start(), calls=%async_computation.7 | async-start | bytes 2654208 | tf_op jit(solution)/shard_map/all_gather | solution.py:155
  200.4 2.1 copy-start.3
  204.6 2.5 copy-start.11
  207.0 70.6 %reduce-scatter.2.cloned.1.call-start = ((), (), s32[]{:S(2)}) async-start(), calls=%async_computation.8 | async-start | bytes 2654208 | tf_op jit(solution)/shard_map/reduce_scatter | solution.py:161
  240.0 0.7 copy-start.8
  240.0 0.7 copy-start.19
  240.0 39.3 %copy-start.5 = (bf16[1152,16]{0,1:T(8,128)(2,1)S(1)}, bf16[1152,16]{0,1:T(8,128)(2,1)}, u32[]{:S(2)}) copy-start(bf16[1152,16]{0,1:T(8,128)(2,1)} %param.52) | copy-start | bytes 110596
  240.7 44.0 %copy-start.15 = (f32[1,4]{1,0:T(1,128)S(1)}, f32[1,4]{1,0:T(1,128)}, u32[]{:S(2)}) copy-start(f32[1,4]{1,0:T(1,128)} %param.35) | copy-start | bytes 52
  240.7 44.0 %copy-start.16 = (f32[1,4]{1,0:T(1,128)S(1)}, f32[1,4]{1,0:T(1,128)}, u32[]{:S(2)}) copy-start(f32[1,4]{1,0:T(1,128)} %param.34) | copy-start | bytes 52
  240.7 44.0 %copy-start.17 = (f32[1,4]{1,0:T(1,128)S(1)}, f32[1,4]{1,0:T(1,128)}, u32[]{:S(2)}) copy-start(f32[1,4]{1,0:T(1,128)} %param.36) | copy-start | bytes 52
  240.7 47.8 %copy-start.9 = (f32[128,8]{0,1:T(8,128)S(1)}, f32[128,8]{0,1:T(8,128)}, u32[]{:S(2)}) copy-start(f32[128,8]{0,1:T(8,128)} %param.30) | copy-start | bytes 12292
  281.4 7.0 %all-to-all-start.3 = ((f32[1,128,16]{1,0,2:T(1,128)}), f32[1,128,16]{1,0,2:T(1,128)S(1)}, u32[]{:S(2)}, u32[]{:S(2)}) async-start(f32[1,128,16]{1,0,2:T(1,128)} %bitcast.21), calls=%async_computation.4 | async-start | bytes 16384 | tf_op jit(solution)/shard_map/all_to_all | solution.py:176
Sparse Core Ops, SparseCore 0:
  9.8 79.4 all-gather.3
  115.4 54.9 all-gather.5
  207.2 24.8 all-gather.7
  240.1 37.4 reduce-scatter.1
where the time goes:
time: 297 us; the launch traced here: 296 us
  waiting for transfers between devices  185 us (62%)
  matrix products  39.1 us (13%)
  local copies, waits for them, and re-layouts  24.1 us (8%)
  starting transfers between devices  21.3 us (7%)
  between operations  13.6 us (5%)
  other arithmetic  12 us (4%)
    all_gather x2, waiting for transfers between devices, split_gather(): lax.all_gather(jnp.concatenate([mine, bias_rows], axis=0), 'req', axis=1,...  106 us
    reduce_scatter x1, waiting for transfers between devices, shards(): lax.psum_scatter(jnp.dot(inner, down_weight, preferred_element_type=jnp.f...  37 us
    all_gather x1, waiting for transfers between devices, shards(): gathered = lax.all_gather(normed_mlp, 'mlp', axis=0, tiled=True)  25 us
    all_gather x2, local copies, waits for them, and re-layouts, split_gather(): lax.all_gather(jnp.concatenate([mine, bias_rows], axis=0), 'req', axis=1,...  10.6 us
    all_to_all x1, starting transfers between devices, shards(): lax.all_to_all(local_mod, 'req', split_axis=0, concat_axis=2, tiled=True)[0]  9.51 us
    sub x1, matrix products, attention(): expo = jnp.where(same, jnp.exp(masked - row_max), 0.0)  8.43 us
    dot_general x1, matrix products, shards(): jnp.dot(inner, down_weight, preferred_element_type=jnp.float32)  7.88 us
    all_to_all x1, waiting for transfers between devices, shards(): lax.all_to_all(local_mod, 'req', split_axis=0, concat_axis=2, tiled=True)[0]  6.92 us
  transfers between devices with their start and end apart: 10, of which 7 were waited for; matrix products, arithmetic and copies ran while one was open for 16% of the time, Pallas kernels for 0%

commit v1 on v0

--- a/solution.py
+++ b/solution.py
@@ -1,3 +1,4 @@
+import functools
 import math
 import jax
 import jax.numpy as jnp
@@ -8,6 +9,16 @@
 HEAD_DIM = 72
 CLASSES = 1000
 FREQ = 256
+
+
+def fix_panel_all(mat, mesh_ax):
+    gallery = []
+    for _ in range(lax.axis_size(mesh_ax)):
+        gallery.append(mat)
+    return jnp.concatenate(lax.all_to_all(jnp.stack(gallery), mesh_ax, 0, 0), axis=0)
+
+
+row_fix = functools.partial(fix_panel_all, mesh_ax="mlp")
 
 
 def layer_norm(values):
@@ -152,7 +163,7 @@
     projected = split_dot(attended, out_mine, out_other)
     mid_hidden = (rows.astype(jnp.float32) + gate_attn * projected).astype(jnp.bfloat16)
     normed_mlp = (layer_norm(mid_hidden) * (1.0 + scale_mlp) + shift_mlp).astype(jnp.bfloat16)
-    gathered = lax.all_gather(normed_mlp, "mlp", axis=0, tiled=True)
+    gathered = row_fix(normed_mlp)
     inner = jax.nn.gelu(
         jnp.dot(gathered, up_weight, preferred_element_type=jnp.float32)
         + up_bias.astype(jnp.float32),

time: 297 us -> 303 us (1.020)
  starting transfers between devices: 21.3 us -> 25.8 us
    all_to_all x0 -> x1, waiting for transfers between devices: none -> 29.9 us  [fix_panel_all(): lax.all_to_all(jnp.stack(gallery), mesh_ax, 0, 0)]
    all_gather x1 -> x0, waiting for transfers between devices: 25 us -> none  [shards(): gathered = lax.all_gather(normed_mlp, 'mlp', axis=0, tiled=True)]
    all_to_all x0 -> x1, starting transfers between devices: none -> 4.5 us  [fix_panel_all(): lax.all_to_all(jnp.stack(gallery), mesh_ax, 0, 0)]
    reduce_scatter x1, waiting for transfers between devices: 37 us -> 33.2 us  [shards(): lax.psum_scatter(jnp.dot(inner, down_weight, preferred_element_type=jnp.f...]
  transfers between devices with their start and end apart: 10 -> 10, of which waited for: 7 -> 7; matrix products, arithmetic and copies ran while one was open for 16% -> 15% of each run, Pallas kernels for 0% -> 0%
where the time goes in v1:
time: 303 us; the launch traced here: 302 us
  waiting for transfers between devices  187 us (62%)
  matrix products  39.1 us (13%)
  local copies, waits for them, and re-layouts  25.9 us (9%)
  starting transfers between devices  25.8 us (9%)
  between operations  13.6 us (4%)
  other arithmetic  11.2 us (4%)
    all_gather x2, waiting for transfers between devices, split_gather(): lax.all_gather(jnp.concatenate([mine, bias_rows], axis=0), 'req', axis=1,...  106 us
    reduce_scatter x1, waiting for transfers between devices, shards(): lax.psum_scatter(jnp.dot(inner, down_weight, preferred_element_type=jnp.f...  33.2 us
    all_to_all x1, waiting for transfers between devices, fix_panel_all(): lax.all_to_all(jnp.stack(gallery), mesh_ax, 0, 0)  29.9 us
    all_gather x2, local copies, waits for them, and re-layouts, split_gather(): lax.all_gather(jnp.concatenate([mine, bias_rows], axis=0), 'req', axis=1,...  10.6 us
    all_to_all x1, starting transfers between devices, shards(): lax.all_to_all(local_mod, 'req', split_axis=0, concat_axis=2, tiled=True)[0]  9.51 us
    sub x1, matrix products, attention(): expo = jnp.where(same, jnp.exp(masked - row_max), 0.0)  8.44 us
    dot_general x1, matrix products, shards(): jnp.dot(inner, down_weight, preferred_element_type=jnp.float32)  7.88 us
    all_to_all x1, waiting for transfers between devices, shards(): lax.all_to_all(local_mod, 'req', split_axis=0, concat_axis=2, tiled=True)[0]  6.91 us
  transfers between devices with their start and end apart: 10, of which 7 were waited for; matrix products, arithmetic and copies ran while one was open for 15% of the time, Pallas kernels for 0%

profile of v1, /device:TPU:8, one launch (start us, length us, event | category | flops | bytes accessed | tf_op | source)
XLA Modules:
  0.0 302.2 jit_solution(4490757149535602058)
XLA Ops:
  6.5 0.9 reshape.221
  7.4 1.1 constant_dynamic-slice_fusion.1
  8.6 0.8 fusion.54
  9.4 0.0 all-gather.3.cloned.1.call-update
  9.5 79.9 %all-gather.3.cloned.1.call-done = bf16[592,3456]{0,1:T(8,128)(2,1)} async-done(((bf16[592,216]{0,1:T(8,128)(2,1)}), bf16[592,3456]{0,1:T(8,128)(2,1)}) %all-gather.3.cloned.1.call-update) | async-done | bytes 4091920 | tf_op jit(solution)/shard_map/all_gather | solution.py:132
  89.3 7.0 %copy.82 = bf16[592,3456]{1,0:T(8,128)(2,1)} copy(bf16[592,3456]{0,1:T(8,128)(2,1)} %all-gather.3.cloned.1.call-done) | data formatting | bytes 8183808 | tf_op jit(solution)/shard_map/all_gather | solution.py:132
  96.4 0.1 copy.78
  96.5 0.1 convert_element_type.93
  96.6 0.1 copy.79
  96.7 0.1 select_n.45
  96.8 0.2 fusion.66
  97.0 1.8 convolution_add_fusion.3
  98.9 3.0 %fusion.37 = bf16[64,576]{1,0:T(8,128)(2,1)S(1)} fusion(bf16[1152,576]{0,1:T(8,128)(2,1)} %param.42, f32[64,1152]{1,0:T(8,128)S(1)} %convolution_add_fusion.3, bf16[1001,1152]{1,0:T(8,128)(2,1)} %param.37, s32[64]{0:T(128)S(1)} %select_n.45, f32[576]{0:T(1024)S(1)} %convert_element_type.98), kind=kOutput, calls=%fused_computation.43 | convolution fusion | flops 233118272 | bytes 4004608 | tf_op jit(solution)/shard_map/dot_general | solution.py:109
  101.9 0.7 reshape.211
  102.6 9.5 %all-to-all-start = ((bf16[16,4,576]{2,1,0:T(4,128)(2,1)}), bf16[16,4,576]{2,1,0:T(4,128)(2,1)S(1)}, u32[]{:S(2)}, u32[]{:S(2)}) async-start(bf16[16,4,576]{2,1,0:T(4,128)(2,1)} %reshape.211), calls=%async_computation | async-start | bytes 163840 | tf_op jit(solution)/shard_map/all_to_all | solution.py:113
  112.1 0.0 all-gather.5.cloned.1.call-start
  112.1 0.1 copy.94
  112.3 0.1 constant_dynamic-slice_fusion
  112.4 0.7 fusion.65
  113.1 0.2 reduce-window.8
  113.3 0.1 convert_reduce_fusion.3
  113.4 0.1 dynamic_slice.21
  113.5 0.1 convert_reduce_fusion.1
  113.6 0.2 fusion.43
  113.9 6.9 %all-to-all-done = bf16[16,4,576]{2,1,0:T(4,128)(2,1)S(1)} async-done(((bf16[16,4,576]{2,1,0:T(4,128)(2,1)}), bf16[16,4,576]{2,1,0:T(4,128)(2,1)S(1)}, u32[]{:S(2)}, u32[]{:S(2)}) %all-to-all-start) | async-done | bytes 73760 | tf_op jit(solution)/shard_map/all_to_all | solution.py:113
  120.8 0.1 squeeze.6
  120.9 0.8 fusion.79
  121.8 2.1 copy-done.1
  123.9 0.3 fusion.46
  124.2 1.8 convert_reduce_fusion
  126.0 3.7 %fusion.4 = f32[128,3456]{1,0:T(8,128)S(1)} fusion(bf16[592,3456]{0,1:T(8,128)(2,1)} %all-gather.3.cloned.1.call-done, bf16[128,1152]{1,0:T(8,128)(2,1)S(1)} %fusion.46, s32[]{:T(128)S(6)} %select_n.47), kind=kOutput, calls=%fused_computation.7 | convolution fusion | flops 509607936 | bytes 6025220 | tf_op jit(solution)/shard_map/dot_general | solution.py:141
  129.7 4.0 %fusion.3 = bf16[128,3456]{1,0:T(8,128)(2,1)} fusion(f32[128,3456]{1,0:T(8,128)S(1)} %fusion.4, bf16[592,3456]{1,0:T(8,128)(2,1)} %collective-permute-done, f32[3456]{0:T(1024)S(1)} %convert_reduce_fusion, bf16[128,1152]{1,0:T(8,128)(2,1)S(1)} %fusion.46, s32[]{:T(128)S(6)} %select_n.48), kind=kOutput, calls=%fused_computation.6 | convolution fusion | flops 510935040 | bytes 6815748 | tf_op jit(solution)/shard_map/dot_general | solution.py:142
  133.8 2.2 copy.83
  136.0 2.1 copy.84
  138.1 4.2 %all-to-all-start.1 = ((bf16[128,8,432]{0,2,1:T(8,128)(2,1)}), bf16[128,8,432]{0,2,1:T(8,128)(2,1)}, u32[]{:S(2)}, u32[]{:S(2)}) async-start(bf16[128,8,432]{0,2,1:T(8,128)(2,1)} %bitcast.97), calls=%async_computation.1 | async-start | bytes 1769472 | tf_op jit(solution)/shard_map/all_to_all | solution.py:154
  142.4 1.7 broadcast_compare_fusion
  144.0 26.4 %all-gather.5.cloned.1.call-done = bf16[592,1152]{0,1:T(8,128)(2,1)} async-done(((bf16[592,72]{0,1:T(8,128)(2,1)}), bf16[592,1152]{0,1:T(8,128)(2,1)}) %all-gather.5.cloned.1.call-update) | async-done | bytes 1363984 | tf_op jit(solution)/shard_map/all_gather | solution.py:132
  170.4 3.6 %copy.89 = bf16[592,1152]{1,0:T(8,128)(2,1)} copy(bf16[592,1152]{0,1:T(8,128)(2,1)} %all-gather.5.cloned.1.call-done) | data formatting | bytes 2727936 | tf_op jit(solution)/shard_map/all_gather | solution.py:132
  174.0 1.3 copy_bitcast_fusion
  175.3 0.8 fusion.98
  176.1 8.4 %fusion.99 = (f32[2,1024]{1,0:T(2,128)S(1)}, bf16[2,1024,1024]{1,2,0:T(8,128)(2,1)}) fusion(pred[1024,1024]{0,1:T(8,128)(4,1)} %broadcast_compare_fusion, bf16[1024,2,72]{0,2,1:T(8,128)(2,1)} %bitcast.105, bf16[1024,2,72]{0,2,1:T(8,128)(2,1)S(1)} %bitcast.104), kind=kOutput, calls=%fused_computation.135 | convolution fusion | flops 314573824 | bytes 5840896 | tf_op jit(solution)/shard_map/sub | solution.py:50
  184.5 3.0 %fusion.34 = bf16[1024,2,72]{0,2,1:T(8,128)(2,1)S(1)} fusion(bf16[1024,2,72]{0,2,1:T(8,128)(2,1)S(1)} %bitcast.103, bf16[2,1024,1024]{1,2,0:T(8,128)(2,1)} %get-tuple-element.40, f32[1024,2]{0,1:T(2,128)S(1)} %bitcast.114), kind=kOutput, calls=%fused_computation.41 | convolution fusion | flops 302284800 | bytes 4792320 | tf_op jit(solution)/shard_map/hqk,khd->qhd/dot_general | solution.py:53
  187.6 0.7 copy.87
  188.4 4.2 %all-to-all-start.2 = ((bf16[8,128,144]{1,2,0:T(8,128)(2,1)}), bf16[8,128,144]{1,2,0:T(8,128)(2,1)S(1)}, u32[]{:S(2)}, u32[]{:S(2)}) async-start(bf16[8,128,144]{1,2,0:T(8,128)(2,1)} %copy.87), calls=%async_computation.2 | async-start | bytes 589824 | tf_op jit(solution)/shard_map/all_to_all | solution.py:162
  192.6 1.2 convert_reduce_fusion.2
  193.8 6.6 %all-to-all-done.2 = bf16[8,128,144]{1,2,0:T(8,128)(2,1)S(1)} async-done(((bf16[8,128,144]{1,2,0:T(8,128)(2,1)}), bf16[8,128,144]{1,2,0:T(8,128)(2,1)S(1)}, u32[]{:S(2)}, u32[]{:S(2)}) %all-to-all-start.2) | async-done | bytes 294944 | tf_op jit(solution)/shard_map/all_to_all | solution.py:162
  200.5 2.1 fusion.25
  202.6 2.1 fusion.100
  204.7 0.2 multiply_reduce_fusion.1
  204.9 1.4 fusion.49
  206.3 1.8 stack.2
  208.1 4.5 %all-to-all-start.3 = ((bf16[8,128,1152]{2,1,0:T(8,128)(2,1)}), bf16[8,128,1152]{2,1,0:T(8,128)(2,1)}, u32[]{:S(2)}, u32[]{:S(2)}) async-start(bf16[8,128,1152]{2,1,0:T(8,128)(2,1)} %stack.2), calls=%async_computation.3 | async-start | bytes 4718592 | tf_op jit(solution)/shard_map/all_to_all | solution.py:18
  212.6 0.0 reduce-scatter.2.cloned.1.call-start
  212.7 29.9 %all-to-all-done.3 = bf16[8,128,1152]{2,1,0:T(8,128)(2,1)} async-done(((bf16[8,128,1152]{2,1,0:T(8,128)(2,1)}), bf16[8,128,1152]{2,1,0:T(8,128)(2,1)}, u32[]{:S(2)}, u32[]{:S(2)}) %all-to-all-start.3) | async-done | bytes 2359328 | tf_op jit(solution)/shard_map/all_to_all | solution.py:18
  242.6 7.9 %convolution_convert_fusion = bf16[1024,1152]{1,0:T(8,128)(2,1)} fusion(bf16[576,1152]{1,0:T(8,128)(2,1)} %param.50, bf16[1024,1152]{1,0:T(8,128)(2,1)} %bitcast.20, bf16[1152,576]{0,1:T(8,128)(2,1)} %param.48, f32[576]{0:T(1024)S(1)} %convert_element_type.107), kind=kOutput, calls=%fused_computation.15 | convolution fusion | flops 2724986880 | bytes 7375104 | tf_op jit(solution)/shard_map/dot_general | solution.py:173
  250.5 0.7 copy-done.8
  251.2 33.2 %reduce-scatter.2.cloned.1.call-done = bf16[128,1152]{1,0:T(8,128)(2,1)} async-done(((bf16[1024,1152]{1,0:T(8,128)(2,1)}), bf16[128,1152]{1,0:T(8,128)(2,1)}) %reduce-scatter.2.cloned.1.call-update) | async-done | bytes 294928 | tf_op jit(solution)/shard_map/reduce_scatter | solution.py:172
  284.3 1.3 fusion.96
  285.7 0.2 multiply_reduce_fusion
  285.9 2.2 convolution_add_fusion.6
  288.1 3.2 %all-to-all-start.4 = ((f32[1,128,16]{1,0,2:T(1,128)}), f32[1,128,16]{1,0,2:T(1,128)S(1)}, u32[]{:S(2)}, u32[]{:S(2)}) async-start(f32[1,128,16]{1,0,2:T(1,128)} %bitcast.22), calls=%async_computation.5 | async-start | bytes 16384 | tf_op jit(solution)/shard_map/all_to_all | solution.py:187
  291.3 0.1 select_reduce_fusion.2
  291.4 3.7 %all-to-all-done.4 = f32[1,128,16]{1,0,2:T(1,128)S(1)} async-done(((f32[1,128,16]{1,0,2:T(1,128)}), f32[1,128,16]{1,0,2:T(1,128)S(1)}, u32[]{:S(2)}, u32[]{:S(2)}) %all-to-all-start.4) | async-done | bytes 8224 | tf_op jit(solution)/shard_map/all_to_all | solution.py:187
  295.1 0.6 fusion.78
  (63 shorter events, 0.3 us)
Async XLA Ops:
  6.5 90.5 %copy-start = (bf16[1152,1152]{1,0:T(8,128)(2,1)S(1)}, bf16[1152,1152]{1,0:T(8,128)(2,1)}, u32[]{:S(2)}) copy-start(bf16[1152,1152]{1,0:T(8,128)(2,1)} %param.40) | copy-start | bytes 7962628
  6.5 82.8 %all-gather.3.cloned.1.call-start = ((), (), s32[]{:S(2)}) async-start(), calls=%async_computation.6 | async-start | bytes 4700160 | tf_op jit(solution)/shard_map/all_gather | solution.py:132
  9.4 87.0 %copy-start.12 = (s32[16,4]{0,1:T(4,128)S(1)}, s32[16,4]{0,1:T(4,128)}, u32[]{:S(2)}) copy-start(s32[16,4]{0,1:T(4,128)} %param.32) | copy-start | bytes 772
  9.4 87.1 %copy-start.6 = (bf16[1152]{0:T(1024)(128)(2,1)S(1)}, bf16[1152]{0:T(1024)(128)(2,1)}, u32[]{:S(2)}) copy-start(bf16[1152]{0:T(1024)(128)(2,1)} %param.39) | copy-start | bytes 6916
  9.4 87.1 %copy-start.7 = (bf16[1152]{0:T(1024)(128)(2,1)S(1)}, bf16[1152]{0:T(1024)(128)(2,1)}, u32[]{:S(2)}) copy-start(bf16[1152]{0:T(1024)(128)(2,1)} %param.41) | copy-start | bytes 6916
  9.4 87.2 %copy-start.13 = (s32[16,4]{0,1:T(4,128)S(1)}, s32[16,4]{0,1:T(4,128)}, u32[]{:S(2)}) copy-start(s32[16,4]{0,1:T(4,128)} %param.31) | copy-start | bytes 772
  9.4 87.3 %copy-start.10 = (bf16[576]{0:T(1024)(128)(2,1)S(1)}, bf16[576]{0:T(1024)(128)(2,1)}, u32[]{:S(2)}) copy-start(bf16[576]{0:T(1024)(128)(2,1)} %param.43) | copy-start | bytes 3460
  96.4 33.3 %collective-permute-start = (bf16[592,3456]{1,0:T(8,128)(2,1)}, bf16[592,3456]{1,0:T(8,128)(2,1)}, u32[]{:S(2)}, u32[]{:S(2)}) collective-permute-start(bf16[592,3456]{1,0:T(8,128)(2,1)} %copy.82), channel_id=1, source_target_pairs={{0,1},{1,0},{2,3},{3,2},{4,5},{5,4},{6,7},{7,6},{8,9},{9,8},{10,11... | collective-permute-start | bytes 12275720 | tf_op jit(solution)/shard_map/ppermute | solution.py:135
  98.8 13.3 %copy-start.14 = (bf16[72]{0:T(256)(128)(2,1)S(1)}, bf16[72]{0:T(256)(128)(2,1)}, u32[]{:S(2)}) copy-start(bf16[72]{0:T(256)(128)(2,1)} %param.47) | copy-start | bytes 436
  98.9 13.4 %copy-start.4 = (bf16[1152,72]{0,1:T(8,128)(2,1)S(1)}, bf16[1152,72]{0,1:T(8,128)(2,1)}, u32[]{:S(2)}) copy-start(bf16[1152,72]{0,1:T(8,128)(2,1)} %param.46) | copy-start | bytes 497668
  98.9 14.3 %copy-start.18 = (s32[1,4]{1,0:T(1,128)S(1)}, s32[1,4]{1,0:T(1,128)}, u32[]{:S(2)}) copy-start(s32[1,4]{1,0:T(1,128)} %param.33) | copy-start | bytes 52
  98.9 14.6 %copy-start.2 = (bf16[1,128,1152]{2,1,0:T(8,128)(2,1)S(1)}, bf16[1,128,1152]{2,1,0:T(8,128)(2,1)}, u32[]{:S(2)}) copy-start(bf16[1,128,1152]{2,1,0:T(8,128)(2,1)} %param.29) | copy-start | bytes 884740
  102.6 18.2 %all-to-all-start = ((bf16[16,4,576]{2,1,0:T(4,128)(2,1)}), bf16[16,4,576]{2,1,0:T(4,128)(2,1)S(1)}, u32[]{:S(2)}, u32[]{:S(2)}) async-start(bf16[16,4,576]{2,1,0:T(4,128)(2,1)} %reshape.211), calls=%async_computation | async-start | bytes 163840 | tf_op jit(solution)/shard_map/all_to_all | solution.py:113
  112.1 58.3 %all-gather.5.cloned.1.call-start = ((), (), s32[]{:S(2)}) async-start(), calls=%async_computation.7 | async-start | bytes 1566720 | tf_op jit(solution)/shard_map/all_gather | solution.py:132
  121.8 2.1 copy-start.1
  138.1 35.9 %all-to-all-start.1 = ((bf16[128,8,432]{0,2,1:T(8,128)(2,1)}), bf16[128,8,432]{0,2,1:T(8,128)(2,1)}, u32[]{:S(2)}, u32[]{:S(2)}) async-start(bf16[128,8,432]{0,2,1:T(8,128)(2,1)} %bitcast.97), calls=%async_computation.1 | async-start | bytes 1769472 | tf_op jit(solution)/shard_map/all_to_all | solution.py:154
  174.0 28.5 %collective-permute-start.1 = (bf16[592,1152]{1,0:T(8,128)(2,1)}, bf16[592,1152]{1,0:T(8,128)(2,1)}, u32[]{:S(2)}, u32[]{:S(2)}) collective-permute-start(bf16[592,1152]{1,0:T(8,128)(2,1)} %copy.89), channel_id=1, source_target_pairs={{0,1},{1,0},{2,3},{3,2},{4,5},{5,4},{6,7},{7,6},{8,9},{9,8},{10,11... | collective-permute-start | bytes 4091912 | tf_op jit(solution)/shard_map/ppermute | solution.py:135
  188.4 12.1 %all-to-all-start.2 = ((bf16[8,128,144]{1,2,0:T(8,128)(2,1)}), bf16[8,128,144]{1,2,0:T(8,128)(2,1)S(1)}, u32[]{:S(2)}, u32[]{:S(2)}) async-start(bf16[8,128,144]{1,2,0:T(8,128)(2,1)} %copy.87), calls=%async_computation.2 | async-start | bytes 589824 | tf_op jit(solution)/shard_map/all_to_all | solution.py:162
  200.5 2.1 copy-start.3
  208.1 4.6 %copy-start.11 = (bf16[576]{0:T(1024)(128)(2,1)S(1)}, bf16[576]{0:T(1024)(128)(2,1)}, u32[]{:S(2)}) copy-start(bf16[576]{0:T(1024)(128)(2,1)} %param.49) | copy-start | bytes 3460
  208.1 34.5 %all-to-all-start.3 = ((bf16[8,128,1152]{2,1,0:T(8,128)(2,1)}), bf16[8,128,1152]{2,1,0:T(8,128)(2,1)}, u32[]{:S(2)}, u32[]{:S(2)}) async-start(bf16[8,128,1152]{2,1,0:T(8,128)(2,1)} %stack.2), calls=%async_computation.3 | async-start | bytes 4718592 | tf_op jit(solution)/shard_map/all_to_all | solution.py:18
  212.6 71.8 %reduce-scatter.2.cloned.1.call-start = ((), (), s32[]{:S(2)}) async-start(), calls=%async_computation.8 | async-start | bytes 2654208 | tf_op jit(solution)/shard_map/reduce_scatter | solution.py:172
  250.5 0.7 copy-start.8
  250.5 0.7 copy-start.19
  250.5 35.5 %copy-start.5 = (bf16[1152,16]{0,1:T(8,128)(2,1)S(1)}, bf16[1152,16]{0,1:T(8,128)(2,1)}, u32[]{:S(2)}) copy-start(bf16[1152,16]{0,1:T(8,128)(2,1)} %param.52) | copy-start | bytes 110596
  251.1 40.2 %copy-start.15 = (f32[1,4]{1,0:T(1,128)S(1)}, f32[1,4]{1,0:T(1,128)}, u32[]{:S(2)}) copy-start(f32[1,4]{1,0:T(1,128)} %param.35) | copy-start | bytes 52
  251.1 40.2 %copy-start.16 = (f32[1,4]{1,0:T(1,128)S(1)}, f32[1,4]{1,0:T(1,128)}, u32[]{:S(2)}) copy-start(f32[1,4]{1,0:T(1,128)} %param.34) | copy-start | bytes 52
  251.1 40.2 %copy-start.17 = (f32[1,4]{1,0:T(1,128)S(1)}, f32[1,4]{1,0:T(1,128)}, u32[]{:S(2)}) copy-start(f32[1,4]{1,0:T(1,128)} %param.36) | copy-start | bytes 52
  251.2 44.0 %copy-start.9 = (f32[128,8]{0,1:T(8,128)S(1)}, f32[128,8]{0,1:T(8,128)}, u32[]{:S(2)}) copy-start(f32[128,8]{0,1:T(8,128)} %param.30) | copy-start | bytes 12292
  288.1 7.0 %all-to-all-start.4 = ((f32[1,128,16]{1,0,2:T(1,128)}), f32[1,128,16]{1,0,2:T(1,128)S(1)}, u32[]{:S(2)}, u32[]{:S(2)}) async-start(f32[1,128,16]{1,0,2:T(1,128)} %bitcast.22), calls=%async_computation.5 | async-start | bytes 16384 | tf_op jit(solution)/shard_map/all_to_all | solution.py:187
Sparse Core Ops, SparseCore 0:
  9.8 79.4 all-gather.2
  115.4 54.9 all-gather.4
  250.6 33.6 reduce-scatter.1
